TPU v7x, 512 devices: a whole 4x8x8 slice. The times are simulated.
512 devices in a mesh: dp: 16 (over y, core), tensor: 32 (over z, x).
Axes of the slice: x: 4, y: 8, z: 8, core: 2. Of those that a mesh axis runs over, the one named last changes fastest.
Arguments:
- layer_input: bfloat16 [65536, 8192], P('dp', 'tensor'), may hold values from -6 to 6
- output_grad: bfloat16 [65536, 1024], P(('dp', 'tensor')), may hold values from -6 to 6
- key_weight: bfloat16 [8192, 1024], P('tensor'), may hold values from -0.0625 to 0.0625
- adapter_down: bfloat16 [128, 16, 8192], P('dp', None, 'tensor'), may hold values from -0.0625 to 0.0625
- adapter_up: bfloat16 [128, 16, 1024], P('dp', None, 'tensor'), may hold values from -0.1875 to 0.1875
- segment_adapter: int32 [512], replicated, may hold values from 0 to 127
- adapter_slot: int32 [128], replicated, may hold values from 0 to 127, each once
- live_segments: int32 [16], P('dp'), may hold values from 1 to 32, as said below
Outputs:
- input_grad: bfloat16 [65536, 8192], P('dp', 'tensor')
- down_grad: bfloat16 [128, 16, 8192], P('dp', None, 'tensor')
- up_grad: bfloat16 [128, 16, 1024], P('dp', None, 'tensor')
Inputs may be any that keep to these rules, and one draw needn't show every extreme that they name: `live_segments`: some data group has all 32 segments live; a group's segments at or past its count are padding.
All inputs are finite; a program needn't handle non-finite values.
Results may differ from a plain program's by a relative error of at most 0.0057.
Values may be sent and summed in bfloat16 or wider, within the bound.
No kernel may reach another device: no remote copies, remote signals or barrier semaphores. Data moves between devices by JAX's collectives and lax.ppermute only.
A program may use at most 64 MiB of HBM per device.

v0:
```python
import jax
import jax.numpy as jnp
from jax import lax
from jax.sharding import PartitionSpec as P


def on_device(
    layer_input,
    output_grad,
    key_weight,
    adapter_down,
    adapter_up,
    segment_adapter,
    adapter_slot,
    live_segments,
):
    tensor_size = lax.axis_size("tensor")
    position = lax.axis_index("tensor")
    group_count = lax.axis_size("dp")
    group_index = lax.axis_index("dp")
    row_count = output_grad.shape[0]
    tok_group = layer_input.shape[0]
    width_shard = layer_input.shape[1]
    key_width = output_grad.shape[1]
    key_shard = key_width // tensor_size
    adapters = adapter_slot.shape[0]
    rank_dim = adapter_down.shape[1]
    per_owner = adapter_down.shape[0]
    seg_total = segment_adapter.shape[0]
    seg_group = seg_total // group_count
    seg_len = tok_group // seg_group
    f32 = jnp.float32
    bf16 = jnp.bfloat16
    whole_raw = lax.all_gather(output_grad, "tensor", axis=0, tiled=True)
    slot_ids = jnp.arange(adapters, dtype=jnp.int32)
    lookup = segment_adapter[:, None] == slot_ids[None, :]
    every_slot = jnp.sum(jnp.where(lookup, adapter_slot[None, :], 0), axis=1)
    seg_slot = lax.dynamic_slice_in_dim(every_slot, group_index * seg_group, seg_group)
    seg_live = jnp.arange(seg_group, dtype=jnp.int32) < live_segments[0]
    local_store = jnp.concatenate([adapter_down, adapter_up], axis=2).reshape(per_owner, -1)
    spread = jnp.broadcast_to(local_store[None], (group_count,) + local_store.shape)
    stores = lax.all_to_all(spread, "dp", 0, 0, tiled=True).reshape(adapters, -1)
    choose = (seg_slot[:, None] == slot_ids[None, :]).astype(bf16)
    seg_store = jnp.dot(choose, stores, preferred_element_type=f32).astype(bf16)
    seg_store = seg_store.reshape(seg_group, rank_dim, width_shard + key_shard)
    down_seg = seg_store[:, :, :width_shard]
    up_seg = seg_store[:, :, width_shard:]
    input_seg = layer_input.reshape(seg_group, seg_len, width_shard)
    proj_part = jnp.einsum("sjd,srd->srj", input_seg, down_seg, preferred_element_type=f32)
    first = jnp.concatenate([proj_part, up_seg.astype(f32)], axis=2).reshape(seg_group, -1)
    first = lax.all_to_all(first, "tensor", 0, 0, tiled=True)
    first = first.reshape(tensor_size, rank_dim, seg_len + key_shard)
    projected_own = jnp.sum(first[:, :, :seg_len], axis=0).astype(bf16)
    up_own = jnp.transpose(first[:, :, seg_len:], (1, 0, 2)).reshape(rank_dim, key_width)
    up_own = up_own.astype(bf16)
    own_live = position < live_segments[0]
    masked_own = jnp.where(own_live, output_grad, jnp.zeros_like(output_grad))
    lowrank_own = lax.dot_general(
        up_own, masked_own, (((1,), (1,)), ((), ())), preferred_element_type=f32
    ).astype(bf16)
    seg_up_own = 2.0 * jnp.dot(projected_own, masked_own, preferred_element_type=f32)
    low_spread = jnp.broadcast_to(
        lowrank_own.reshape(1, row_count * rank_dim), (tensor_size, row_count * rank_dim)
    )
    up_pieces = jnp.transpose(
        seg_up_own.reshape(rank_dim, tensor_size, key_shard), (1, 0, 2)
    ).reshape(tensor_size, rank_dim * key_shard)
    up_round = lax.reduce_precision(up_pieces, exponent_bits=8, mantissa_bits=7)
    up_high = up_round.astype(bf16)
    up_low = (up_pieces - up_round).astype(bf16)
    second = jnp.concatenate([low_spread, up_high, up_low], axis=1)
    second = second.reshape(tensor_size, -1, 128)
    second = lax.all_to_all(second, "tensor", 0, 0, tiled=True).reshape(tensor_size, -1)
    lowrank = second[:, : row_count * rank_dim].reshape(seg_group, rank_dim, seg_len)
    piece = rank_dim * key_shard
    low_end = row_count * rank_dim
    seg_up = second[:, low_end : low_end + piece].astype(f32)
    seg_up = seg_up + second[:, low_end + piece :].astype(f32)
    seg_up = seg_up.reshape(seg_group, rank_dim, key_shard)
    seg_down = 2.0 * jnp.einsum("srj,sjd->srd", lowrank, input_seg, preferred_element_type=f32)
    seg_grad = jnp.concatenate([seg_down, seg_up], axis=2)
    onehot = (slot_ids[:, None] == seg_slot[None, :]).astype(bf16)
    grad_round = lax.reduce_precision(seg_grad, exponent_bits=8, mantissa_bits=7)
    grad_high = grad_round.astype(bf16)
    grad_low = (seg_grad - grad_round).astype(bf16)
    flat_high = grad_high.reshape(seg_group, -1)
    flat_low = grad_low.reshape(seg_group, -1)
    part = jnp.dot(onehot, flat_high, preferred_element_type=f32)
    part = part + jnp.dot(onehot, flat_low, preferred_element_type=f32)
    part = part.astype(bf16).reshape(group_count, per_owner, -1)
    gathered = lax.all_to_all(part, "dp", 0, 0, tiled=True)
    frozen = lax.dot_general(
        whole_raw, key_weight, (((1,), (1,)), ((), ())), preferred_element_type=f32
    )
    frozen = jnp.where(jnp.repeat(seg_live, seg_len)[:, None], frozen, jnp.zeros_like(frozen))
    extra = jnp.einsum("srj,srd->sjd", lowrank, down_seg, preferred_element_type=f32)
    input_grad = (frozen + 2.0 * extra.reshape(tok_group, width_shard)).astype(bf16)
    gathered, input_grad = lax.optimization_barrier((gathered, input_grad))
    total = jnp.sum(gathered.astype(f32), axis=0).reshape(per_owner, rank_dim, -1)
    down_grad = total[:, :, :width_shard].astype(bf16)
    up_grad = total[:, :, width_shard:].astype(bf16)
    return (input_grad, down_grad, up_grad)


def solution(mesh):
    in_specs = (
        P("dp", "tensor"),
        P(("dp", "tensor"), None),
        P("tensor", None),
        P("dp", None, "tensor"),
        P("dp", None, "tensor"),
        P(),
        P(),
        P("dp"),
    )
    out_specs = (P("dp", "tensor"), P("dp", None, "tensor"), P("dp", None, "tensor"))
    return jax.shard_map(
        on_device, mesh=mesh, in_specs=in_specs, out_specs=out_specs, check_vma=False
    )
```

profile of v0, /device:TPU:1, one launch (start us, length us, event | category | flops | bytes accessed | tf_op | source)
XLA Modules:
  0.0 147.1 jit_solution(13841824733136216324)
XLA Ops:
  7.2 0.0 copy-start
  7.2 0.0 copy-start.5
  7.2 0.0 copy-start.6
  7.2 0.0 all-gather.2.cloned.1.call-start
  7.2 0.7 all-gather.2.cloned.1.call-update
  7.9 0.9 pad_maximum_fusion.2
  8.8 0.1 broadcast_in_dim.54
  9.0 1.1 broadcast_in_dim.55
  10.0 10.4 %all-to-all-start = ((bf16[16,8,4608]{2,1,0:T(8,128)(2,1)}), bf16[16,8,4608]{2,1,0:T(8,128)(2,1)S(1)}, u32[]{:S(2)}, u32[]{:S(2)}) async-start(bf16[16,8,4608]{2,1,0:T(8,128)(2,1)} %broadcast_in_dim.55), calls=%async_computation | async-start | bytes 2359296 | tf_op jit(solution)/shard_map/all_to_all | solution.py:42
  20.4 0.0 copy-done.5
  20.4 0.0 copy-done.6
  20.4 0.2 select_reduce_fusion
  20.7 0.1 dynamic_slice.3
  20.7 30.3 %all-to-all-done = bf16[16,8,4608]{2,1,0:T(8,128)(2,1)S(1)} async-done(((bf16[16,8,4608]{2,1,0:T(8,128)(2,1)}), bf16[16,8,4608]{2,1,0:T(8,128)(2,1)S(1)}, u32[]{:S(2)}, u32[]{:S(2)}) %all-to-all-start) | async-done | bytes 1179680 | tf_op jit(solution)/shard_map/all_to_all | solution.py:42
  51.0 1.1 convolution_convert_fusion
  52.1 1.5 %reshape.65 = bf16[32,16,288]{2,1,0:T(8,128)(2,1)S(1)} reshape(bf16[32,4608]{1,0:T(8,128)(2,1)} %convolution_convert_fusion) | data formatting | bytes 589824 | tf_op jit(solution)/shard_map/reshape | solution.py:45
  53.6 0.0 copy-start.1
  53.6 0.0 copy-done
  53.7 0.6 fusion.10
  54.3 0.0 copy-start.4
  54.3 0.1 pad_maximum_fusion.1
  54.4 1.4 all_to_all.20
  55.8 0.0 copy-done.1
  55.8 11.1 %all-to-all-start.1 = ((f32[32,1,2560]{2,1,0:T(1,128)}), f32[32,1,2560]{2,1,0:T(1,128)S(1)}, u32[]{:S(2)}, u32[]{:S(2)}) async-start(f32[32,1,2560]{2,1,0:T(1,128)} %all_to_all.20), calls=%async_computation.1 | async-start | bytes 655360 | tf_op jit(solution)/shard_map/all_to_all | solution.py:51
  67.5 13.1 %all-to-all-done.1 = f32[32,1,2560]{2,1,0:T(1,128)S(1)} async-done(((f32[32,1,2560]{2,1,0:T(1,128)}), f32[32,1,2560]{2,1,0:T(1,128)S(1)}, u32[]{:S(2)}, u32[]{:S(2)}) %all-to-all-start.1) | async-done | bytes 327712 | tf_op jit(solution)/shard_map/all_to_all | solution.py:51
  80.6 0.8 reduce.1
  81.4 0.3 reshape.67
  81.7 0.0 copy-done.4
  81.7 0.2 convolution_multiply_fusion.2
  81.9 0.1 reshape.68
  82.0 0.2 copy.25
  82.2 0.1 reshape.69
  82.4 0.2 convert_element_type.55
  82.6 0.2 fusion.5
  82.8 16.6 %all_to_all.25 = bf16[32,24,128]{2,1,0:T(8,128)(2,1)S(1)} all-to-all(bf16[32,24,128]{2,1,0:T(8,128)(2,1)S(1)} %bitcast.45), channel_id=1, replica_groups=mesh['dp'=16,'tensor'=32] {'tensor'}, dimensions={0} | all-to-all | bytes 393216 | tf_op jit(solution)/shard_map/all_to_all | solution.py:73
  99.5 0.0 copy-start.2
  99.6 0.1 reshape.73
  99.7 0.4 convolution_multiply_fusion.1
  100.1 0.1 copy-done.2
  100.2 0.1 pad_maximum_fusion
  100.2 0.3 concatenate.18
  100.6 0.4 fusion.8
  101.0 0.0 copy-start.3
  101.0 1.6 %fusion.1 = bf16[16,8,4608]{2,1,0:T(8,128)(2,1)} fusion(f32[128,4608]{1,0:T(8,128)S(1)} %fusion.8, f32[32,4608]{1,0:T(8,128)S(1)} %concatenate.18, s32[32]{0:T(128)S(1)} %dynamic_slice.3), kind=kOutput, calls=%fused_computation.2 | convolution fusion | flops 39374848 | bytes 4128896 | tf_op jit(solution)/shard_map/dot_general | solution.py:89
  102.6 5.5 %all-to-all-start.3 = ((bf16[16,8,4608]{2,1,0:T(8,128)(2,1)}), bf16[16,8,4608]{2,1,0:T(8,128)(2,1)S(1)}, u32[]{:S(2)}, u32[]{:S(2)}) async-start(bf16[16,8,4608]{2,1,0:T(8,128)(2,1)} %fusion.1), calls=%async_computation.3 | async-start | bytes 2359296 | tf_op jit(solution)/shard_map/all_to_all | solution.py:91
  108.1 0.1 broadcast_bitcast_fusion
  108.2 0.0 copy-done.3
  108.2 3.7 %convolution_multiply_fusion = f32[32,128,256]{2,1,0:T(8,128)} fusion(bf16[32,16,128]{2,1,0:T(8,128)(2,1)S(1)} %bitcast.41, bf16[32,16,288]{2,1,0:T(8,128)(2,1)} %copy-done.1), kind=kOutput, calls=%fused_computation.7 | convolution fusion | flops 34603008 | bytes 4587520 | tf_op jit(solution)/shard_map/srj,srd->sjd/dot_general | solution.py:96
  111.8 13.0 %all-gather.2.cloned.1.call-done = bf16[4096,1024]{1,0:T(8,128)(2,1)} async-done(((bf16[128,1024]{1,0:T(8,128)(2,1)}), bf16[4096,1024]{1,0:T(8,128)(2,1)}) %all-gather.2.cloned.1.call-update) | async-done | bytes 8388624 | tf_op jit(solution)/shard_map/all_gather | solution.py:34
  124.9 7.1 %fusion.3 = bf16[4096,256]{1,0:T(8,128)(2,1)} fusion(f32[4096,256]{1,0:T(8,128)} %bitcast.39, bf16[4096,1024]{1,0:T(8,128)(2,1)} %all-gather.2.cloned.1.call-done, bf16[256,1024]{1,0:T(8,128)(2,1)} %param.10, pred[4096]{0:T(1024)(128)(4,1)S(1)} %broadcast_bitcast_fusion), kind=kOutput, calls=%fused_computation.6 | convolution fusion | flops 2150629376 | bytes 15208448 | tf_op jit(solution)/shard_map/dot_general | solution.py:92
  131.9 6.7 %all-to-all-done.3 = bf16[16,8,4608]{2,1,0:T(8,128)(2,1)S(1)} async-done(((bf16[16,8,4608]{2,1,0:T(8,128)(2,1)}), bf16[16,8,4608]{2,1,0:T(8,128)(2,1)S(1)}, u32[]{:S(2)}, u32[]{:S(2)}) %all-to-all-start.3) | async-done | bytes 1179680 | tf_op jit(solution)/shard_map/all_to_all | solution.py:91
  138.7 0.2 reduce
  138.8 0.2 reshape.76
  139.0 0.6 slice.46
  139.7 0.6 slice.47
  (13 shorter events, 0.3 us)
Async XLA Ops:
  7.2 46.5 %copy-start = (bf16[4096,256]{1,0:T(8,128)(2,1)S(1)}, bf16[4096,256]{1,0:T(8,128)(2,1)}, u32[]{:S(2)}) copy-start(bf16[4096,256]{1,0:T(8,128)(2,1)} %param.8) | copy-start | bytes 6291460
  7.2 13.2 %copy-start.5 = (s32[512]{0:T(512)S(1)}, s32[512]{0:T(512)}, u32[]{:S(2)}) copy-start(s32[512]{0:T(512)} %param.13) | copy-start | bytes 6148
  7.2 13.2 %copy-start.6 = (s32[128]{0:T(128)S(1)}, s32[128]{0:T(128)}, u32[]{:S(2)}) copy-start(s32[128]{0:T(128)} %param.14) | copy-start | bytes 1540
  7.2 117.7 %all-gather.2.cloned.1.call-start = ((), (), s32[]{:S(2)}) async-start(), calls=%async_computation.4 | async-start | bytes 8650752 | tf_op jit(solution)/shard_map/all_gather | solution.py:34
  10.0 41.0 %all-to-all-start = ((bf16[16,8,4608]{2,1,0:T(8,128)(2,1)}), bf16[16,8,4608]{2,1,0:T(8,128)(2,1)S(1)}, u32[]{:S(2)}, u32[]{:S(2)}) async-start(bf16[16,8,4608]{2,1,0:T(8,128)(2,1)} %broadcast_in_dim.55), calls=%async_computation | async-start | bytes 2359296 | tf_op jit(solution)/shard_map/all_to_all | solution.py:42
  53.6 2.2 %copy-start.1 = (bf16[32,16,288]{2,1,0:T(8,128)(2,1)}, bf16[32,16,288]{2,1,0:T(8,128)(2,1)S(1)}, u32[]{:S(2)}) copy-start(bf16[32,16,288]{2,1,0:T(8,128)(2,1)S(1)} %reshape.65) | copy-start | bytes 884740
  54.3 27.4 %copy-start.4 = (bf16[128,1024]{1,0:T(8,128)(2,1)S(1)}, bf16[128,1024]{1,0:T(8,128)(2,1)}, u32[]{:S(2)}) copy-start(bf16[128,1024]{1,0:T(8,128)(2,1)} %param.9) | copy-start | bytes 786436
  55.8 24.9 %all-to-all-start.1 = ((f32[32,1,2560]{2,1,0:T(1,128)}), f32[32,1,2560]{2,1,0:T(1,128)S(1)}, u32[]{:S(2)}, u32[]{:S(2)}) async-start(f32[32,1,2560]{2,1,0:T(1,128)} %all_to_all.20), calls=%async_computation.1 | async-start | bytes 655360 | tf_op jit(solution)/shard_map/all_to_all | solution.py:51
  99.5 0.6 copy-start.2
  101.0 7.1 %copy-start.3 = (bf16[4,8,16,128]{3,2,1,0:T(8,128)(2,1)S(1)}, bf16[4,8,16,128]{3,2,1,0:T(8,128)(2,1)}, u32[]{:S(2)}) copy-start(bf16[4,8,16,128]{3,2,1,0:T(8,128)(2,1)} %copy-done.2) | copy-start | bytes 393220
  102.6 36.1 %all-to-all-start.3 = ((bf16[16,8,4608]{2,1,0:T(8,128)(2,1)}), bf16[16,8,4608]{2,1,0:T(8,128)(2,1)S(1)}, u32[]{:S(2)}, u32[]{:S(2)}) async-start(bf16[16,8,4608]{2,1,0:T(8,128)(2,1)} %fusion.1), calls=%async_computation.3 | async-start | bytes 2359296 | tf_op jit(solution)/shard_map/all_to_all | solution.py:91
Sparse Core Ops, SparseCore 0:
  11.2 113.6 all-gather.1
where the time goes:
time: 148 us; the launch traced here: 147 us
  waiting for transfers between devices  63.8 us (43%)
  starting transfers between devices  27 us (18%)
  blocking collectives  16.6 us (11%)
  matrix products  15.2 us (10%)
  between operations  14.9 us (10%)
  local copies, waits for them, and re-layouts  7.34 us (5%)
  other arithmetic  2.28 us (2%)
    all_to_all x1, waiting for transfers between devices, on_device(): lax.all_to_all(spread, 'dp', 0, 0, tiled=True).reshape(adapters, -1)  30.3 us
    all_to_all x1, blocking collectives, on_device(): lax.all_to_all(second, 'tensor', 0, 0, tiled=True).reshape(tensor_size, -1)  16.6 us
    all_to_all x1, waiting for transfers between devices, on_device(): first = lax.all_to_all(first, 'tensor', 0, 0, tiled=True)  13.1 us
    all_gather x1, waiting for transfers between devices, on_device(): whole_raw = lax.all_gather(output_grad, 'tensor', axis=0, tiled=True)  13 us
    all_to_all x1, starting transfers between devices, on_device(): first = lax.all_to_all(first, 'tensor', 0, 0, tiled=True)  11.1 us
    all_to_all x1, starting transfers between devices, on_device(): lax.all_to_all(spread, 'dp', 0, 0, tiled=True).reshape(adapters, -1)  10.4 us
    dot_general x1, matrix products, on_device(): lax.dot_general(whole_raw, key_weight, (((1,), (1,)), ((), ())), preferre...  7.09 us
    all_to_all x1, waiting for transfers between devices, on_device(): gathered = lax.all_to_all(part, 'dp', 0, 0, tiled=True)  6.74 us
  transfers between devices with their start and end apart: 4, of which 4 were waited for; matrix products, arithmetic and copies ran while one was open for 15% of the time, Pallas kernels for 0%

commit v1 on v0

--- a/solution.py
+++ b/solution.py
@@ -2,6 +2,7 @@
 import jax.numpy as jnp
 from jax import lax
 from jax.sharding import PartitionSpec as P
+from jax.lax import all_to_all, psum
 
 
 def on_device(
@@ -31,7 +32,8 @@
     seg_len = tok_group // seg_group
     f32 = jnp.float32
     bf16 = jnp.bfloat16
-    whole_raw = lax.all_gather(output_grad, "tensor", axis=0, tiled=True)
+    v_next = jnp.concatenate(psum(1, "tensor") * [output_grad], 0)
+    whole_raw = all_to_all(v_next, "tensor", 0, 0, tiled=True)
     slot_ids = jnp.arange(adapters, dtype=jnp.int32)
     lookup = segment_adapter[:, None] == slot_ids[None, :]
     every_slot = jnp.sum(jnp.where(lookup, adapter_slot[None, :], 0), axis=1)

time: 148 us -> 325 us (2.20)
  waiting for transfers between devices: 63.8 us -> 229 us
  local copies, waits for them, and re-layouts: 7.34 us -> 41.7 us
  blocking collectives: 16.6 us -> 0 us
  between operations: 14.9 us -> 1.51 us
  starting transfers between devices: 27 us -> 35.5 us
    all_to_all x0 -> x2, waiting for transfers between devices: none -> 192 us  [the longest x1 185 us: on_device(): whole_raw = all_to_all(v_next, 'tensor', 0, 0, tiled=True)]
    unnamed x18 -> x41, local copies, waits for them, and re-layouts: 0.22 us -> 31.8 us
    all_to_all x1, waiting for transfers between devices: 30.3 us -> 5.09 us  [on_device(): lax.all_to_all(spread, 'dp', 0, 0, tiled=True).reshape(adapters, -1)]
    all_to_all x1 -> x0, blocking collectives: 16.6 us -> none  [on_device(): lax.all_to_all(second, 'tensor', 0, 0, tiled=True).reshape(tensor_size, -1)]
    all_to_all x1, waiting for transfers between devices: 6.74 us -> 22.8 us  [on_device(): gathered = lax.all_to_all(part, 'dp', 0, 0, tiled=True)]
    all_gather x1 -> x0, waiting for transfers between devices: 13 us -> none  [on_device(): whole_raw = lax.all_gather(output_grad, 'tensor', axis=0, tiled=True)]
    all_to_all x0 -> x2, starting transfers between devices: none -> 9.08 us  [the longest x1 4.96 us: on_device(): whole_raw = all_to_all(v_next, 'tensor', 0, 0, tiled=True)]
    all_to_all x1, waiting for transfers between devices: 13.1 us -> 8.75 us  [on_device(): first = lax.all_to_all(first, 'tensor', 0, 0, tiled=True)]
  transfers between devices with their start and end apart: 4 -> 5, of which waited for: 4 -> 5; matrix products, arithmetic and copies ran while one was open for 15% -> 14% of each run, Pallas kernels for 0% -> 0%
where the time goes in v1:
time: 325 us; the launch traced here: 324 us
  waiting for transfers between devices  229 us (70%)
  local copies, waits for them, and re-layouts  41.7 us (13%)
  starting transfers between devices  35.5 us (11%)
  matrix products  12.1 us (4%)
  other arithmetic  4.78 us (1%)
    all_to_all x1, waiting for transfers between devices, on_device(): whole_raw = all_to_all(v_next, 'tensor', 0, 0, tiled=True)  185 us
    unnamed x41, local copies, waits for them, and re-layouts  31.8 us
    all_to_all x1, waiting for transfers between devices, on_device(): gathered = lax.all_to_all(part, 'dp', 0, 0, tiled=True)  22.8 us
    all_to_all x1, starting transfers between devices, on_device(): first = lax.all_to_all(first, 'tensor', 0, 0, tiled=True)  11.1 us
    all_to_all x1, starting transfers between devices, on_device(): lax.all_to_all(spread, 'dp', 0, 0, tiled=True).reshape(adapters, -1)  10.4 us
    all_to_all x1, waiting for transfers between devices, on_device(): first = lax.all_to_all(first, 'tensor', 0, 0, tiled=True)  8.75 us
    all_to_all x1, waiting for transfers between devices, on_device(): lax.all_to_all(second, 'tensor', 0, 0, tiled=True).reshape(tensor_size, -1)  7.72 us
  transfers between devices with their start and end apart: 5, of which 5 were waited for; matrix products, arithmetic and copies ran while one was open for 14% of the time, Pallas kernels for 0%

profile of v1, /device:TPU:1, one launch (start us, length us, event | category | flops | bytes accessed | tf_op | source)
XLA Modules:
  0.0 324.4 jit_solution(16047105888117839680)
XLA Ops:
  0.7 1.0 pad_maximum_fusion.2
  1.8 1.1 broadcast_in_dim.55
  2.9 10.4 %all-to-all-start = ((bf16[16,8,4608]{2,1,0:T(8,128)(2,1)}), bf16[16,8,4608]{2,1,0:T(8,128)(2,1)S(1)}, u32[]{:S(2)}, u32[]{:S(2)}) async-start(bf16[16,8,4608]{2,1,0:T(8,128)(2,1)} %broadcast_in_dim.55), calls=%async_computation | async-start | bytes 2359296 | tf_op jit(solution)/shard_map/all_to_all | solution.py:44
  13.3 1.7 constant_dynamic-update-slice_fusion.31
  15.0 1.7 constant_dynamic-update-slice_fusion.30
  16.7 1.7 constant_dynamic-update-slice_fusion.29
  18.3 0.9 select_reduce_fusion
  19.3 1.7 constant_dynamic-update-slice_fusion.28
  21.0 1.7 constant_dynamic-update-slice_fusion.27
  22.7 1.7 constant_dynamic-update-slice_fusion.26
  24.4 1.7 constant_dynamic-update-slice_fusion.25
  26.1 1.7 constant_dynamic-update-slice_fusion.24
  27.7 1.7 constant_dynamic-update-slice_fusion.23
  29.4 0.7 constant_dynamic-update-slice_fusion.22
  30.1 0.7 constant_dynamic-update-slice_fusion.21
  30.9 0.7 constant_dynamic-update-slice_fusion.20
  31.6 0.7 constant_dynamic-update-slice_fusion.19
  32.3 0.7 constant_dynamic-update-slice_fusion.18
  33.0 0.7 constant_dynamic-update-slice_fusion.17
  33.7 0.7 constant_dynamic-update-slice_fusion.16
  34.5 0.7 constant_dynamic-update-slice_fusion.15
  35.2 0.7 constant_dynamic-update-slice_fusion.14
  35.9 0.7 constant_dynamic-update-slice_fusion.13
  36.6 0.7 constant_dynamic-update-slice_fusion.12
  37.4 0.7 constant_dynamic-update-slice_fusion.11
  38.1 0.7 constant_dynamic-update-slice_fusion.10
  38.8 5.1 %all-to-all-done = bf16[16,8,4608]{2,1,0:T(8,128)(2,1)S(1)} async-done(((bf16[16,8,4608]{2,1,0:T(8,128)(2,1)}), bf16[16,8,4608]{2,1,0:T(8,128)(2,1)S(1)}, u32[]{:S(2)}, u32[]{:S(2)}) %all-to-all-start) | async-done | bytes 1179680 | tf_op jit(solution)/shard_map/all_to_all | solution.py:44
  43.9 1.1 convolution_convert_fusion
  45.0 1.5 reshape.67
  46.5 0.6 fusion.10
  47.2 1.4 all_to_all.31
  48.6 11.1 %all-to-all-start.1 = ((f32[32,1,2560]{2,1,0:T(1,128)}), f32[32,1,2560]{2,1,0:T(1,128)S(1)}, u32[]{:S(2)}, u32[]{:S(2)}) async-start(f32[32,1,2560]{2,1,0:T(1,128)} %all_to_all.31), calls=%async_computation.1 | async-start | bytes 655360 | tf_op jit(solution)/shard_map/all_to_all | solution.py:53
  59.7 0.7 constant_dynamic-update-slice_fusion.9
  61.1 0.7 constant_dynamic-update-slice_fusion.8
  61.8 0.7 constant_dynamic-update-slice_fusion.7
  62.5 0.7 constant_dynamic-update-slice_fusion.6
  63.3 0.7 constant_dynamic-update-slice_fusion.5
  64.0 0.7 constant_dynamic-update-slice_fusion.4
  64.7 8.7 %all-to-all-done.1 = f32[32,1,2560]{2,1,0:T(1,128)S(1)} async-done(((f32[32,1,2560]{2,1,0:T(1,128)}), f32[32,1,2560]{2,1,0:T(1,128)S(1)}, u32[]{:S(2)}, u32[]{:S(2)}) %all-to-all-start.1) | async-done | bytes 327712 | tf_op jit(solution)/shard_map/all_to_all | solution.py:53
  73.5 1.5 reduce.1
  75.0 1.3 reshape.69
  77.0 0.2 convert_element_type.55
  77.1 0.2 fusion.5
  77.4 0.7 copy.20
  78.1 4.1 %all-to-all-start.2 = ((bf16[32,24,128]{2,1,0:T(8,128)(2,1)}), bf16[32,24,128]{2,1,0:T(8,128)(2,1)S(1)}, u32[]{:S(2)}, u32[]{:S(2)}) async-start(bf16[32,24,128]{2,1,0:T(8,128)(2,1)} %bitcast.12), calls=%async_computation.2 | async-start | bytes 393216 | tf_op jit(solution)/shard_map/all_to_all | solution.py:75
  82.2 0.7 constant_dynamic-update-slice_fusion.3
  82.9 0.7 constant_dynamic-update-slice_fusion.2
  83.6 0.7 constant_dynamic-update-slice_fusion.1
  84.4 0.7 constant_dynamic-update-slice_fusion
  85.1 7.7 %all-to-all-done.2 = bf16[32,24,128]{2,1,0:T(8,128)(2,1)S(1)} async-done(((bf16[32,24,128]{2,1,0:T(8,128)(2,1)}), bf16[32,24,128]{2,1,0:T(8,128)(2,1)S(1)}, u32[]{:S(2)}, u32[]{:S(2)}) %all-to-all-start.2) | async-done | bytes 196640 | tf_op jit(solution)/shard_map/all_to_all | solution.py:75
  92.8 5.0 %all-to-all-start.4 = ((bf16[32,128,1024]{2,1,0:T(8,128)(2,1)}), bf16[32,128,1024]{2,1,0:T(8,128)(2,1)}, u32[]{:S(2)}, u32[]{:S(2)}) async-start(bf16[32,128,1024]{2,1,0:T(8,128)(2,1)} %bitcast.8), calls=%async_computation.4 | async-start | bytes 16777216 | tf_op jit(solution)/shard_map/all_to_all | solution.py:36
  98.0 0.4 convolution_multiply_fusion.1
  98.4 0.9 pad_maximum_fusion
  99.4 1.4 concatenate.21
  100.8 0.4 fusion.8
  101.2 1.5 fusion.1
  102.7 184.5 %all-to-all-done.4 = bf16[32,128,1024]{2,1,0:T(8,128)(2,1)} async-done(((bf16[32,128,1024]{2,1,0:T(8,128)(2,1)}), bf16[32,128,1024]{2,1,0:T(8,128)(2,1)}, u32[]{:S(2)}, u32[]{:S(2)}) %all-to-all-start.4) | async-done | bytes 8388640 | tf_op jit(solution)/shard_map/all_to_all | solution.py:36
  287.2 5.0 %all-to-all-start.3 = ((bf16[16,8,4608]{2,1,0:T(8,128)(2,1)}), bf16[16,8,4608]{2,1,0:T(8,128)(2,1)S(1)}, u32[]{:S(2)}, u32[]{:S(2)}) async-start(bf16[16,8,4608]{2,1,0:T(8,128)(2,1)} %fusion.1), calls=%async_computation.3 | async-start | bytes 2359296 | tf_op jit(solution)/shard_map/all_to_all | solution.py:93
  292.3 1.7 convolution_multiply_fusion
  294.0 6.0 %fusion.3 = bf16[4096,256]{1,0:T(8,128)(2,1)} fusion(f32[4096,256]{1,0:T(8,128)S(1)} %bitcast.41, bf16[4096,1024]{1,0:T(8,128)(2,1)} %bitcast.9, bf16[256,1024]{1,0:T(8,128)(2,1)} %param.10, pred[4096]{0:T(1024)(128)(4,1)S(1)} %broadcast_bitcast_fusion), kind=kOutput, calls=%fused_computation.6 | convolution fusion | flops 2150629376 | bytes 15208448 | tf_op jit(solution)/shard_map/dot_general | solution.py:94
  300.1 22.8 %all-to-all-done.3 = bf16[16,8,4608]{2,1,0:T(8,128)(2,1)S(1)} async-done(((bf16[16,8,4608]{2,1,0:T(8,128)(2,1)}), bf16[16,8,4608]{2,1,0:T(8,128)(2,1)S(1)}, u32[]{:S(2)}, u32[]{:S(2)}) %all-to-all-start.3) | async-done | bytes 1179680 | tf_op jit(solution)/shard_map/all_to_all | solution.py:93
  323.0 0.2 reshape.78
  323.2 0.6 slice.46
  323.8 0.6 slice.47
  (28 shorter events, 1.5 us)
Async XLA Ops:
  0.6 45.9 %copy-start = (bf16[4096,256]{1,0:T(8,128)(2,1)S(1)}, bf16[4096,256]{1,0:T(8,128)(2,1)}, u32[]{:S(2)}) copy-start(bf16[4096,256]{1,0:T(8,128)(2,1)} %param.8) | copy-start | bytes 6291460
  0.6 28.8 %copy-start.1 = (bf16[128,1024]{1,0:T(8,128)(2,1)S(1)}, bf16[128,1024]{1,0:T(8,128)(2,1)}, u32[]{:S(2)}) copy-start(bf16[128,1024]{1,0:T(8,128)(2,1)} %param.9) | copy-start | bytes 786436
  2.9 41.0 %all-to-all-start = ((bf16[16,8,4608]{2,1,0:T(8,128)(2,1)}), bf16[16,8,4608]{2,1,0:T(8,128)(2,1)S(1)}, u32[]{:S(2)}, u32[]{:S(2)}) async-start(bf16[16,8,4608]{2,1,0:T(8,128)(2,1)} %broadcast_in_dim.55), calls=%async_computation | async-start | bytes 2359296 | tf_op jit(solution)/shard_map/all_to_all | solution.py:44
  46.5 46.4 %copy-start.2 = (bf16[32,16,288]{2,1,0:T(8,128)(2,1)}, bf16[32,16,288]{2,1,0:T(8,128)(2,1)S(1)}, u32[]{:S(2)}) copy-start(bf16[32,16,288]{2,1,0:T(8,128)(2,1)S(1)} %reshape.67) | copy-start | bytes 884740
  48.6 24.9 %all-to-all-start.1 = ((f32[32,1,2560]{2,1,0:T(1,128)}), f32[32,1,2560]{2,1,0:T(1,128)S(1)}, u32[]{:S(2)}, u32[]{:S(2)}) async-start(f32[32,1,2560]{2,1,0:T(1,128)} %all_to_all.31), calls=%async_computation.1 | async-start | bytes 655360 | tf_op jit(solution)/shard_map/all_to_all | solution.py:53
  78.1 14.8 %all-to-all-start.2 = ((bf16[32,24,128]{2,1,0:T(8,128)(2,1)}), bf16[32,24,128]{2,1,0:T(8,128)(2,1)S(1)}, u32[]{:S(2)}, u32[]{:S(2)}) async-start(bf16[32,24,128]{2,1,0:T(8,128)(2,1)} %bitcast.12), calls=%async_computation.2 | async-start | bytes 393216 | tf_op jit(solution)/shard_map/all_to_all | solution.py:75
  92.8 194.4 %all-to-all-start.4 = ((bf16[32,128,1024]{2,1,0:T(8,128)(2,1)}), bf16[32,128,1024]{2,1,0:T(8,128)(2,1)}, u32[]{:S(2)}, u32[]{:S(2)}) async-start(bf16[32,128,1024]{2,1,0:T(8,128)(2,1)} %bitcast.8), calls=%async_computation.4 | async-start | bytes 16777216 | tf_op jit(solution)/shard_map/all_to_all | solution.py:36
  287.2 35.6 %all-to-all-start.3 = ((bf16[16,8,4608]{2,1,0:T(8,128)(2,1)}), bf16[16,8,4608]{2,1,0:T(8,128)(2,1)S(1)}, u32[]{:S(2)}, u32[]{:S(2)}) async-start(bf16[16,8,4608]{2,1,0:T(8,128)(2,1)} %fusion.1), calls=%async_computation.3 | async-start | bytes 2359296 | tf_op jit(solution)/shard_map/all_to_all | solution.py:93
